TPU v7x, 512 devices: a whole 4x8x8 slice. The times are simulated.
512 devices in a mesh: req: 64 (over y, x, core), tp: 8 (over z).
Axes of the slice: x: 4, y: 8, z: 8, core: 2. Of those that a mesh axis runs over, the one named last changes fastest.
Arguments:
- tokens: bfloat16 [8192, 8192], P('req', 'tp'), may hold values from -6 to 6
- kv_weight: bfloat16 [8192, 1024], P('tp'), may hold values from -0.0625 to 0.0625
- queries: bfloat16 [8192, 4096], P('req', 'tp'), may hold values from -96 to 96, as said below
- lengths: int32 [32], replicated, may hold values from 1 to 384, 8192 in all
- page_owner: int32 [4096, 1], P('req'), may hold values from 0 to 63; in each aligned block of 64 rows (0 to 63, 64 to 127, ...) at most 2 rows name the same one
Outputs:
- attended: bfloat16 [8192, 4096], P('req', 'tp')
- cache: bfloat16 [16384, 1024], P('req', 'tp')
Inputs may be any that keep to these rules, and one draw needn't show every extreme that they name: `queries`: real values; entries of a row share a scale. The 32 lengths sum to 8192; the largest is exactly 384. `page_owner`: among the 64 pages of one device no owner is named more than 2 times, a bound that some block reaches.
All inputs are finite; a program needn't handle non-finite values.
Results may differ from a plain program's by a relative error of at most 0.012.
Values may be sent and summed in bfloat16 or wider, within the bound.
No kernel may reach another device: no remote copies, remote signals or barrier semaphores. Data moves between devices by JAX's collectives and lax.ppermute only.
A program may use at most 64 MiB of HBM per device.

v0:
```python
import math
import jax
import jax.numpy as jnp
from jax import lax
from jax.sharding import PartitionSpec as P

HD = 128
HQ = 32
KVH = 4
BACK = 3
rope_base = 500000.0


def shifted(value, axis, steps):
    count = lax.axis_size(axis)
    first, last = (max(0, -steps), min(count, count - steps))
    return lax.ppermute(value, axis, [(source, source + steps) for source in range(first, last)])


def rotate(values, positions):
    middle = HD // 2
    frequency = rope_base ** (-(2.0 * jnp.arange(middle, dtype=jnp.float32)) / HD)
    angles = positions.astype(jnp.float32)[:, None] * frequency[None, :]
    cosine = jnp.cos(angles)[:, None, :]
    sine = jnp.sin(angles)[:, None, :]
    front = values[..., :middle]
    behind = values[..., middle:]
    return jnp.concatenate(
        [front * cosine - behind * sine, behind * cosine + front * sine], axis=-1
    )


def rotate_keys(block, positions):
    rows = block.shape[0]
    parts = block.shape[1] // HD
    shaped = block.reshape(rows, parts, HD)
    turned = rotate(shaped, positions)
    is_key = jnp.arange(parts, dtype=jnp.int32) % 2 == 0
    return jnp.where(is_key[None, :, None], turned, shaped).reshape(rows, parts * HD)


def segment_info(lengths, indices):
    ends = jnp.cumsum(lengths)
    before = ends[None, :] <= indices[:, None]
    segment = jnp.sum(before.astype(jnp.int32), axis=1)
    start = jnp.sum(jnp.where(before, lengths[None, :], 0), axis=1)
    return (segment, indices - start)


def local(tokens, kv_weight, queries, lengths, page_owner):
    rows = tokens.shape[0]
    columns = kv_weight.shape[1]
    share = columns // lax.axis_size("tp")
    tp_index = lax.axis_index("tp")
    req_index = lax.axis_index("req")
    local_index = req_index * rows + jnp.arange(rows, dtype=jnp.int32)
    segment, positions = segment_info(lengths, local_index)
    local_heads = queries.shape[1] // HD
    group = HQ // KVH
    per_group = min(local_heads, group)
    kv_count = local_heads // per_group
    first_head = tp_index * local_heads // group
    partial_value = jnp.dot(tokens, kv_weight, preferred_element_type=jnp.float32)
    summed = lax.psum(partial_value, "tp")
    cache_rows = rotate_keys(summed, positions).astype(jnp.bfloat16)
    mine = lax.dynamic_slice_in_dim(cache_rows, tp_index * share, share, 1)
    near = lax.dynamic_slice_in_dim(cache_rows, first_head * 2 * HD, kv_count * 2 * HD, 1)
    rotated = rotate(queries.astype(jnp.float32).reshape(rows, local_heads, HD), positions).astype(
        jnp.bfloat16
    )
    blocks = []
    for distance in range(BACK, 0, -1):
        blocks.append(shifted(near, "req", distance))
    blocks.append(near)
    window = jnp.concatenate(blocks, axis=0)
    key_total = (BACK + 1) * rows
    key_index = (req_index - BACK) * rows + jnp.arange(key_total, dtype=jnp.int32)
    key_segment, unused = segment_info(lengths, key_index)
    allowed = (
        (key_index[None, :] >= 0)
        & (key_index[None, :] <= local_index[:, None])
        & (key_segment[None, :] == segment[:, None])
    )
    key_parts = window.reshape(key_total, kv_count, 2, HD)
    head_keys = jnp.transpose(key_parts[:, :, 0, :], (1, 0, 2))
    head_values = jnp.transpose(key_parts[:, :, 1, :], (1, 0, 2))
    query_heads = jnp.transpose(rotated, (1, 0, 2))

    def attend_head(head):
        query_head = query_heads[head]
        slot = head // per_group
        key_head = head_keys[slot]
        value_head = head_values[slot]
        scores = lax.dot_general(
            query_head, key_head, (((1,), (1,)), ((), ())), preferred_element_type=jnp.float32
        ) / math.sqrt(HD)
        scores = jnp.where(allowed, scores, -1e30)
        largest = jnp.max(scores, axis=1, keepdims=True)
        weights = jnp.exp(scores - largest)
        total = jnp.sum(weights, axis=1, keepdims=True)
        mixed = jnp.dot(
            weights.astype(jnp.bfloat16), value_head, preferred_element_type=jnp.float32
        )
        return (mixed / total).astype(jnp.bfloat16)

    outputs = lax.map(attend_head, jnp.arange(local_heads, dtype=jnp.int32))
    attended = jnp.transpose(outputs, (1, 0, 2)).reshape(rows, local_heads * HD)
    pages_here = page_owner.shape[0]
    owners = page_owner[:, 0]
    page_rows = rows // pages_here
    capacity = 2 * pages_here // lax.axis_size("req")
    order = jnp.arange(pages_here, dtype=jnp.int32)
    earlier = (owners[:, None] == owners[None, :]) & (order[None, :] < order[:, None])
    rank = jnp.sum(earlier.astype(jnp.int32), axis=1)
    target = owners * capacity + rank
    slots = lax.axis_size("req") * capacity
    placing = (jnp.arange(slots, dtype=jnp.int32)[:, None] == target[None, :]).astype(jnp.bfloat16)
    paged = mine.reshape(pages_here, page_rows * share)
    outgoing = jnp.dot(placing, paged, preferred_element_type=jnp.float32).astype(jnp.bfloat16)
    incoming = lax.all_to_all(outgoing, "req", split_axis=0, concat_axis=0, tiled=True)
    cache = incoming.reshape(slots * page_rows, share)
    return (attended, cache)


def solution(mesh):
    in_specs = (P("req", "tp"), P("tp", None), P("req", "tp"), P(), P("req", None))
    out_specs = (P("req", "tp"), P("req", "tp"))
    return jax.shard_map(local, mesh=mesh, in_specs=in_specs, out_specs=out_specs, check_vma=False)
```

profile of v0, /device:TPU:1, one launch (start us, length us, event | category | flops | bytes accessed | tf_op | source)
XLA Modules:
  0.0 141.3 jit_solution(10183100208050448432)
XLA Ops:
  7.3 1.5 %copy-done = bf16[1024,1024]{1,0:T(8,128)(2,1)S(1)} copy-done((bf16[1024,1024]{1,0:T(8,128)(2,1)S(1)}, bf16[1024,1024]{1,0:T(8,128)(2,1)}, u32[]{:S(2)}) %copy-start) | copy-done | bytes 2097176
  8.8 2.2 %fusion.23 = f32[128,1024]{1,0:T(8,128)} fusion(bf16[128,1024]{1,0:T(8,128)(2,1)} %param.7, bf16[1024,1024]{1,0:T(8,128)(2,1)S(1)} %copy-done), kind=kOutput, calls=%fused_computation.54 | convolution fusion | flops 268435456 | bytes 2883584 | tf_op jit(solution)/shard_map/dot_general | solution.py:63
  12.5 79.8 %all-reduce.2.cloned.1.call-done = f32[128,1024]{1,0:T(8,128)} async-done(((f32[128,1024]{1,0:T(8,128)}), f32[128,1024]{1,0:T(8,128)}) %all-reduce.2.cloned.1.call-update) | async-done | bytes 524304 | tf_op jit(solution)/shard_map/psum | solution.py:64
  92.2 1.2 copy.31
  93.5 0.3 multiply_subtract_fusion
  94.0 9.6 %collective-permute-start = (bf16[128,256]{1,0:T(8,128)(2,1)S(1)}, bf16[128,256]{1,0:T(8,128)(2,1)S(1)}, u32[]{:S(2)}, u32[]{:S(2)}) collective-permute-start(bf16[128,256]{1,0:T(8,128)(2,1)S(1)} %constant_dynamic-slice_fusion.1), channel_id=1, source_target_pairs={{0,24},{8,32},{16,40},{24,48},{32,56},{40,64},{48,72},{56,80},{64,... | collective-permute-start | bytes 196616 | tf_op jit(solution)/shard_map/ppermute | solution.py:17
  103.6 2.2 %collective-permute-start.1 = (bf16[128,256]{1,0:T(8,128)(2,1)S(1)}, bf16[128,256]{1,0:T(8,128)(2,1)S(1)}, u32[]{:S(2)}, u32[]{:S(2)}) collective-permute-start(bf16[128,256]{1,0:T(8,128)(2,1)S(1)} %constant_dynamic-slice_fusion.1), channel_id=1, source_target_pairs={{0,16},{8,24},{16,32},{24,40},{32,48},{40,56},{48,64},{56,72},{64,... | collective-permute-start | bytes 196616 | tf_op jit(solution)/shard_map/ppermute | solution.py:17
  105.8 1.9 %collective-permute-start.2 = (bf16[128,256]{1,0:T(8,128)(2,1)S(1)}, bf16[128,256]{1,0:T(8,128)(2,1)S(1)}, u32[]{:S(2)}, u32[]{:S(2)}) collective-permute-start(bf16[128,256]{1,0:T(8,128)(2,1)S(1)} %constant_dynamic-slice_fusion.1), channel_id=1, source_target_pairs={{0,8},{8,16},{16,24},{24,32},{32,40},{40,48},{48,56},{56,64},{64,7... | collective-permute-start | bytes 196616 | tf_op jit(solution)/shard_map/ppermute | solution.py:17
  107.9 0.7 all_to_all.6
  108.6 9.9 %all-to-all-start = ((bf16[64,2,256]{2,1,0:T(2,128)(2,1)}), bf16[64,2,256]{2,1,0:T(2,128)(2,1)S(1)}, u32[]{:S(2)}, u32[]{:S(2)}) async-start(bf16[64,2,256]{2,1,0:T(2,128)(2,1)} %all_to_all.6), calls=%async_computation | async-start | bytes 131072 | tf_op jit(solution)/shard_map/all_to_all | solution.py:120
  118.6 0.4 fusion.22
  119.0 14.1 %while.11 = (s32[]{:T(128)}, bf16[4,128,128]{2,1,0:T(8,128)(2,1)S(1)}, s32[4]{0:T(128)S(1)}, bf16[4,128,128]{1,2,0:T(8,128)(2,1)S(1)}, bf16[1,512,128]{2,1,0:T(8...) while((s32[]{:T(128)}, ...), condition=%wide.region_8.9_spmd.clone, body=%wide.region_5.8_spmd.clone.sunk | while | flops 34307844 | bytes 1122491 | solution.py:106
  119.1 0.7 dynamic_slice.30
  121.8 0.3 fusion.35
  122.3 0.3 fusion.37
  122.6 0.7 dynamic_slice.30
  125.3 0.3 fusion.35
  125.8 0.3 fusion.37
  126.1 0.7 dynamic_slice.30
  128.8 0.3 fusion.35
  129.6 0.7 dynamic_slice.30
  132.4 0.3 fusion.35
  133.1 0.7 copy_bitcast_fusion
  133.8 0.7 reshape.163
  (53 shorter events, 3.2 us)
Async XLA Ops:
  7.2 1.6 %copy-start = (bf16[1024,1024]{1,0:T(8,128)(2,1)S(1)}, bf16[1024,1024]{1,0:T(8,128)(2,1)}, u32[]{:S(2)}) copy-start(bf16[1024,1024]{1,0:T(8,128)(2,1)} %param.8) | copy-start | bytes 6291460
  7.2 3.9 %copy-start.3 = (s32[32]{0:T(128)S(1)}, s32[32]{0:T(128)}, u32[]{:S(2)}) copy-start(s32[32]{0:T(128)} %param.10) | copy-start | bytes 388
  7.2 4.7 %copy-start.2 = (bf16[128,512]{1,0:T(8,128)(2,1)S(1)}, bf16[128,512]{1,0:T(8,128)(2,1)}, u32[]{:S(2)}) copy-start(bf16[128,512]{1,0:T(8,128)(2,1)} %param.9) | copy-start | bytes 393220
  7.2 5.0 %copy-start.4 = (s32[64,1]{0,1:T(1,128)S(1)}, s32[64,1]{0,1:T(1,128)}, u32[]{:S(2)}) copy-start(s32[64,1]{0,1:T(1,128)} %param.11) | copy-start | bytes 772
  7.2 85.0 %all-reduce.2.cloned.1.call-start = ((), (), s32[]{:S(2)}) async-start(), calls=%async_computation.1 | async-start | bytes 1048576 | tf_op jit(solution)/shard_map/psum | solution.py:64
  92.2 1.6 %copy-start.1 = (f32[128,1024]{1,0:T(8,128)S(1)}, f32[128,1024]{1,0:T(8,128)}, u32[]{:S(2)}) copy-start(f32[128,1024]{1,0:T(8,128)} %all-reduce.2.cloned.1.call-done) | copy-start | bytes 1572868
  94.0 24.5 %collective-permute-start = (bf16[128,256]{1,0:T(8,128)(2,1)S(1)}, bf16[128,256]{1,0:T(8,128)(2,1)S(1)}, u32[]{:S(2)}, u32[]{:S(2)}) collective-permute-start(bf16[128,256]{1,0:T(8,128)(2,1)S(1)} %constant_dynamic-slice_fusion.1), channel_id=1, source_target_pairs={{0,24},{8,32},{16,40},{24,48},{32,56},{40,64},{48,72},{56,80},{64,... | collective-permute-start | bytes 196616 | tf_op jit(solution)/shard_map/ppermute | solution.py:17
  103.6 14.9 %collective-permute-start.1 = (bf16[128,256]{1,0:T(8,128)(2,1)S(1)}, bf16[128,256]{1,0:T(8,128)(2,1)S(1)}, u32[]{:S(2)}, u32[]{:S(2)}) collective-permute-start(bf16[128,256]{1,0:T(8,128)(2,1)S(1)} %constant_dynamic-slice_fusion.1), channel_id=1, source_target_pairs={{0,16},{8,24},{16,32},{24,40},{32,48},{40,56},{48,64},{56,72},{64,... | collective-permute-start | bytes 196616 | tf_op jit(solution)/shard_map/ppermute | solution.py:17
  105.8 12.7 %collective-permute-start.2 = (bf16[128,256]{1,0:T(8,128)(2,1)S(1)}, bf16[128,256]{1,0:T(8,128)(2,1)S(1)}, u32[]{:S(2)}, u32[]{:S(2)}) collective-permute-start(bf16[128,256]{1,0:T(8,128)(2,1)S(1)} %constant_dynamic-slice_fusion.1), channel_id=1, source_target_pairs={{0,8},{8,16},{16,24},{24,32},{32,40},{40,48},{48,56},{56,64},{64,7... | collective-permute-start | bytes 196616 | tf_op jit(solution)/shard_map/ppermute | solution.py:17
  108.6 25.2 %all-to-all-start = ((bf16[64,2,256]{2,1,0:T(2,128)(2,1)}), bf16[64,2,256]{2,1,0:T(2,128)(2,1)S(1)}, u32[]{:S(2)}, u32[]{:S(2)}) async-start(bf16[64,2,256]{2,1,0:T(2,128)(2,1)} %all_to_all.6), calls=%async_computation | async-start | bytes 131072 | tf_op jit(solution)/shard_map/all_to_all | solution.py:120
Sparse Core Ops, SparseCore 0:
  11.1 81.0 all-reduce.1
where the time goes:
time: 142 us; the launch traced here: 141 us
  waiting for transfers between devices  79.8 us (56%)
  starting transfers between devices  23.6 us (17%)
  between operations  14.4 us (10%)
  local copies, waits for them, and re-layouts  8.42 us (6%)
  loops' own time  8.37 us (6%)
  matrix products  4.61 us (3%)
  other arithmetic  2.13 us (2%)
    psum x1, waiting for transfers between devices, local(): summed = lax.psum(partial_value, 'tp')  79.8 us
    ppermute x3, starting transfers between devices, shifted(): lax.ppermute(value, axis, [(source, source + steps) for source in range(f...  13.7 us
    all_to_all x1, starting transfers between devices, local(): lax.all_to_all(outgoing, 'req', split_axis=0, concat_axis=0, tiled=True)  9.92 us
    another operation x1, loops' own time, local(): outputs = lax.map(attend_head, jnp.arange(local_heads, dtype=jnp.int32))  8.37 us
    unnamed x12, local copies, waits for them, and re-layouts  2.86 us
  transfers between devices with their start and end apart: 5, of which 1 were waited for; matrix products, arithmetic and copies ran while one was open for 6% of the time, Pallas kernels for 0%

commit v1 on v0

--- a/solution.py
+++ b/solution.py
@@ -61,7 +61,7 @@
     kv_count = local_heads // per_group
     first_head = tp_index * local_heads // group
     partial_value = jnp.dot(tokens, kv_weight, preferred_element_type=jnp.float32)
-    summed = lax.psum(partial_value, "tp")
+    summed = jnp.sum(lax.all_gather(partial_value, "tp"), axis=0)
     cache_rows = rotate_keys(summed, positions).astype(jnp.bfloat16)
     mine = lax.dynamic_slice_in_dim(cache_rows, tp_index * share, share, 1)
     near = lax.dynamic_slice_in_dim(cache_rows, first_head * 2 * HD, kv_count * 2 * HD, 1)

time: 142 us -> 121 us (0.85)
  waiting for transfers between devices: 79.8 us -> 62.2 us
  starting transfers between devices: 23.6 us -> 19.4 us
  other arithmetic: 2.13 us -> 4.74 us
    psum x1 -> x0, waiting for transfers between devices: 79.8 us -> none  [local(): summed = lax.psum(partial_value, 'tp')]
    all_gather x0 -> x1, waiting for transfers between devices: none -> 62.2 us  [local(): summed = jnp.sum(lax.all_gather(partial_value, 'tp'), axis=0)]
    ppermute x3, starting transfers between devices: 13.7 us -> 9.56 us  [shifted(): lax.ppermute(value, axis, [(source, source + steps) for source in range(f...]
    reduce_sum x0 -> x1, other arithmetic: none -> 2.61 us  [local(): summed = jnp.sum(lax.all_gather(partial_value, 'tp'), axis=0)]
  transfers between devices with their start and end apart: 5 -> 5, of which waited for: 1 -> 1; matrix products, arithmetic and copies ran while one was open for 6% -> 7% of each run, Pallas kernels for 0% -> 0%
where the time goes in v1:
time: 121 us
  waiting for transfers between devices  62.2 us (51%)
  starting transfers between devices  19.4 us (16%)
  between operations  14.4 us (12%)
  loops' own time  8.37 us (7%)
  local copies, waits for them, and re-layouts  7.23 us (6%)
  other arithmetic  4.74 us (4%)
  matrix products  4.59 us (4%)
    all_gather x1, waiting for transfers between devices, local(): summed = jnp.sum(lax.all_gather(partial_value, 'tp'), axis=0)  62.2 us
    all_to_all x1, starting transfers between devices, local(): lax.all_to_all(outgoing, 'req', split_axis=0, concat_axis=0, tiled=True)  9.81 us
    ppermute x3, starting transfers between devices, shifted(): lax.ppermute(value, axis, [(source, source + steps) for source in range(f...  9.56 us
    another operation x1, loops' own time, local(): outputs = lax.map(attend_head, jnp.arange(local_heads, dtype=jnp.int32))  8.37 us
    dynamic_slice x4, local copies, waits for them, and re-layouts, local(): outputs = lax.map(attend_head, jnp.arange(local_heads, dtype=jnp.int32))  2.67 us
    reduce_sum x1, other arithmetic, local(): summed = jnp.sum(lax.all_gather(partial_value, 'tp'), axis=0)  2.61 us
  transfers between devices with their start and end apart: 5, of which 1 were waited for; matrix products, arithmetic and copies ran while one was open for 7% of the time, Pallas kernels for 0%

profile of v1, /device:TPU:1, one launch (start us, length us, event | category | flops | bytes accessed | tf_op | source)
XLA Modules:
  0.0 120.9 jit_solution(12185984456571214890)
XLA Ops:
  7.3 1.5 %copy-done = bf16[1024,1024]{1,0:T(8,128)(2,1)S(1)} copy-done((bf16[1024,1024]{1,0:T(8,128)(2,1)S(1)}, bf16[1024,1024]{1,0:T(8,128)(2,1)}, u32[]{:S(2)}) %copy-start) | copy-done | bytes 2097176
  8.8 2.2 %fusion.22 = f32[128,1024]{1,0:T(8,128)} fusion(bf16[128,1024]{1,0:T(8,128)(2,1)} %param.7, bf16[1024,1024]{1,0:T(8,128)(2,1)S(1)} %copy-done), kind=kOutput, calls=%fused_computation.53 | convolution fusion | flops 268435456 | bytes 2883584 | tf_op jit(solution)/shard_map/dot_general | solution.py:63
  12.5 62.2 %all-gather.3.cloned.1.call-done = f32[1024,1024]{1,0:T(8,128)} async-done(((f32[128,1024]{1,0:T(8,128)}), f32[1024,1024]{1,0:T(8,128)}) %all-gather.3.cloned.1.call-update) | async-done | bytes 4194320 | tf_op jit(solution)/shard_map/all_gather | solution.py:64
  74.6 2.6 %reduce_sum.55 = f32[128,1024]{1,0:T(8,128)S(1)} reduce(f32[8,128,1024]{2,1,0:T(8,128)} %bitcast.62, f32[]{:T(128)} %constant.85.clone.1), dimensions={0}, to_apply=%region_2.3 | reduce | flops 917504 | bytes 4718596 | tf_op jit(solution)/shard_map/reduce_sum | solution.py:64
  77.3 0.3 multiply_subtract_fusion
  77.9 5.3 %collective-permute-start = (bf16[128,256]{1,0:T(8,128)(2,1)S(1)}, bf16[128,256]{1,0:T(8,128)(2,1)S(1)}, u32[]{:S(2)}, u32[]{:S(2)}) collective-permute-start(bf16[128,256]{1,0:T(8,128)(2,1)S(1)} %constant_dynamic-slice_fusion.1), channel_id=1, source_target_pairs={{0,24},{8,32},{16,40},{24,48},{32,56},{40,64},{48,72},{56,80},{64,... | collective-permute-start | bytes 196616 | tf_op jit(solution)/shard_map/ppermute | solution.py:17
  83.2 2.2 %collective-permute-start.1 = (bf16[128,256]{1,0:T(8,128)(2,1)S(1)}, bf16[128,256]{1,0:T(8,128)(2,1)S(1)}, u32[]{:S(2)}, u32[]{:S(2)}) collective-permute-start(bf16[128,256]{1,0:T(8,128)(2,1)S(1)} %constant_dynamic-slice_fusion.1), channel_id=1, source_target_pairs={{0,16},{8,24},{16,32},{24,40},{32,48},{40,56},{48,64},{56,72},{64,... | collective-permute-start | bytes 196616 | tf_op jit(solution)/shard_map/ppermute | solution.py:17
  85.4 2.0 %collective-permute-start.2 = (bf16[128,256]{1,0:T(8,128)(2,1)S(1)}, bf16[128,256]{1,0:T(8,128)(2,1)S(1)}, u32[]{:S(2)}, u32[]{:S(2)}) collective-permute-start(bf16[128,256]{1,0:T(8,128)(2,1)S(1)} %constant_dynamic-slice_fusion.1), channel_id=1, source_target_pairs={{0,8},{8,16},{16,24},{24,32},{32,40},{40,48},{48,56},{56,64},{64,7... | collective-permute-start | bytes 196616 | tf_op jit(solution)/shard_map/ppermute | solution.py:17
  87.6 0.7 all_to_all.6
  88.3 9.8 %all-to-all-start = ((bf16[64,2,256]{2,1,0:T(2,128)(2,1)}), bf16[64,2,256]{2,1,0:T(2,128)(2,1)S(1)}, u32[]{:S(2)}, u32[]{:S(2)}) async-start(bf16[64,2,256]{2,1,0:T(2,128)(2,1)} %all_to_all.6), calls=%async_computation | async-start | bytes 131072 | tf_op jit(solution)/shard_map/all_to_all | solution.py:120
  98.6 14.1 %while.11 = (s32[]{:T(128)}, bf16[4,128,128]{2,1,0:T(8,128)(2,1)S(1)}, s32[4]{0:T(128)S(1)}, bf16[4,128,128]{1,2,0:T(8,128)(2,1)S(1)}, bf16[1,512,128]{2,1,0:T(8...) while((s32[]{:T(128)}, ...), condition=%wide.region_8.9_spmd.clone, body=%wide.region_5.8_spmd.clone.sunk | while | flops 34307844 | bytes 1122491 | solution.py:106
  98.6 0.7 dynamic_slice.30
  101.4 0.3 fusion.34
  101.9 0.3 fusion.36
  102.2 0.7 dynamic_slice.30
  104.9 0.3 fusion.34
  105.4 0.3 fusion.36
  105.7 0.7 dynamic_slice.30
  108.4 0.3 fusion.34
  108.9 0.3 fusion.36
  109.2 0.7 dynamic_slice.30
  111.9 0.3 fusion.34
  112.7 0.7 copy_bitcast_fusion
  113.4 0.7 reshape.163
  (53 shorter events, 3.4 us)
Async XLA Ops:
  7.2 1.6 %copy-start = (bf16[1024,1024]{1,0:T(8,128)(2,1)S(1)}, bf16[1024,1024]{1,0:T(8,128)(2,1)}, u32[]{:S(2)}) copy-start(bf16[1024,1024]{1,0:T(8,128)(2,1)} %param.8) | copy-start | bytes 6291460
  7.2 3.8 %copy-start.2 = (s32[32]{0:T(128)S(1)}, s32[32]{0:T(128)}, u32[]{:S(2)}) copy-start(s32[32]{0:T(128)} %param.10) | copy-start | bytes 388
  7.2 4.6 %copy-start.1 = (bf16[128,512]{1,0:T(8,128)(2,1)S(1)}, bf16[128,512]{1,0:T(8,128)(2,1)}, u32[]{:S(2)}) copy-start(bf16[128,512]{1,0:T(8,128)(2,1)} %param.9) | copy-start | bytes 393220
  7.2 4.8 %copy-start.3 = (s32[64,1]{0,1:T(1,128)S(1)}, s32[64,1]{0,1:T(1,128)}, u32[]{:S(2)}) copy-start(s32[64,1]{0,1:T(1,128)} %param.11) | copy-start | bytes 772
  7.2 67.4 %all-gather.3.cloned.1.call-start = ((), (), s32[]{:S(2)}) async-start(), calls=%async_computation.1 | async-start | bytes 4718592 | tf_op jit(solution)/shard_map/all_gather | solution.py:64
  77.9 20.3 %collective-permute-start = (bf16[128,256]{1,0:T(8,128)(2,1)S(1)}, bf16[128,256]{1,0:T(8,128)(2,1)S(1)}, u32[]{:S(2)}, u32[]{:S(2)}) collective-permute-start(bf16[128,256]{1,0:T(8,128)(2,1)S(1)} %constant_dynamic-slice_fusion.1), channel_id=1, source_target_pairs={{0,24},{8,32},{16,40},{24,48},{32,56},{40,64},{48,72},{56,80},{64,... | collective-permute-start | bytes 196616 | tf_op jit(solution)/shard_map/ppermute | solution.py:17
  83.2 14.9 %collective-permute-start.1 = (bf16[128,256]{1,0:T(8,128)(2,1)S(1)}, bf16[128,256]{1,0:T(8,128)(2,1)S(1)}, u32[]{:S(2)}, u32[]{:S(2)}) collective-permute-start(bf16[128,256]{1,0:T(8,128)(2,1)S(1)} %constant_dynamic-slice_fusion.1), channel_id=1, source_target_pairs={{0,16},{8,24},{16,32},{24,40},{32,48},{40,56},{48,64},{56,72},{64,... | collective-permute-start | bytes 196616 | tf_op jit(solution)/shard_map/ppermute | solution.py:17
  85.4 12.7 %collective-permute-start.2 = (bf16[128,256]{1,0:T(8,128)(2,1)S(1)}, bf16[128,256]{1,0:T(8,128)(2,1)S(1)}, u32[]{:S(2)}, u32[]{:S(2)}) collective-permute-start(bf16[128,256]{1,0:T(8,128)(2,1)S(1)} %constant_dynamic-slice_fusion.1), channel_id=1, source_target_pairs={{0,8},{8,16},{16,24},{24,32},{32,40},{40,48},{48,56},{56,64},{64,7... | collective-permute-start | bytes 196616 | tf_op jit(solution)/shard_map/ppermute | solution.py:17
  88.3 25.1 %all-to-all-start = ((bf16[64,2,256]{2,1,0:T(2,128)(2,1)}), bf16[64,2,256]{2,1,0:T(2,128)(2,1)S(1)}, u32[]{:S(2)}, u32[]{:S(2)}) async-start(bf16[64,2,256]{2,1,0:T(2,128)(2,1)} %all_to_all.6), calls=%async_computation | async-start | bytes 131072 | tf_op jit(solution)/shard_map/all_to_all | solution.py:120
Sparse Core Ops, SparseCore 0:
  11.1 63.4 all-gather.2
